TPU v7x, 32 devices: a whole 2x2x4 slice. The times are simulated.
32 devices in a mesh: ctx: 4 (over y, core), row: 8 (over z, x).
Axes of the slice: x: 2, y: 2, z: 4, core: 2. Of those that a mesh axis runs over, the one named last changes fastest.
Arguments:
- queries: bfloat16 [16, 2, 4096], P('row'), may hold values from -400 to 400
- prefix_id: int32 [16], P('row'), may hold values from 0 to 7
- prefix_keys: bfloat16 [8, 1024, 512], P(None, ('ctx', 'row')), may hold values from -8 to 8
- prefix_values: bfloat16 [8, 1024, 512], P(None, ('ctx', 'row')), may hold values from -6 to 6
- pool_keys: bfloat16 [512, 64, 512], P(('ctx', 'row')), may hold values from -5 to 5
- pool_values: bfloat16 [512, 64, 512], P(('ctx', 'row')), may hold values from -6 to 6
- page_table: int32 [16, 32], P('row'), may hold values from 0 to 511, as said below
- suffix_len: int32 [16], P('row'), may hold values from 256 to 2048
- new_keys: bfloat16 [16, 2, 512], P('row'), may hold values from -6.25 to 6.25
- new_values: bfloat16 [16, 2, 512], P('row'), may hold values from -6 to 6
Outputs:
- attended: bfloat16 [16, 2, 4096], P('row')
Inputs may be any that keep to these rules, and one draw needn't show every extreme that they name: `page_table`: the 64 entries of the rows i with one value of i // 2 name different pool pages p with (p // 16) % (8) == i // 2, and together they name all such pages.
All inputs are finite; a program needn't handle non-finite values.
Results may differ from a plain program's by a relative error of at most 0.003.
Values may be sent and summed in bfloat16 or wider, within the bound.
No kernel may reach another device: no remote copies, remote signals or barrier semaphores. Data moves between devices by JAX's collectives and lax.ppermute only.
A program may use at most 64 MiB of HBM per device.

v0:
```python
import math
import jax
import jax.numpy as jnp
from jax import lax
from jax.sharding import PartitionSpec as P

H = 32
KVH = 4
HD = 128
LANES = 128
MASKED_SCORE = -1e30


def block_stats(scores, valid_mask, values, einsum_form):
    block_peak = jnp.max(jnp.where(valid_mask, scores, MASKED_SCORE), axis=-1)
    weights = jnp.where(valid_mask, jnp.exp(scores - block_peak[..., None]), 0.0).astype(
        jnp.bfloat16
    )
    block_total = jnp.sum(weights.astype(jnp.float32), axis=-1)
    block_sum = jnp.einsum(einsum_form, weights, values, preferred_element_type=jnp.float32)
    return (block_peak, block_total, block_sum)


def combine_pair(earlier, later):
    highest = jnp.maximum(earlier[0], later[0])
    left_factor = jnp.exp(earlier[0] - highest)
    right_factor = jnp.exp(later[0] - highest)
    totals = left_factor * earlier[1] + right_factor * later[1]
    sums = left_factor[..., None] * earlier[2] + right_factor[..., None] * later[2]
    return (highest, totals, sums)


def per_device(
    queries,
    prefix_id,
    prefix_keys,
    prefix_values,
    pool_keys,
    pool_values,
    page_table,
    suffix_len,
    new_keys,
    new_values,
):
    rows_dev, step_count, feature_width = queries.shape
    groups = H // KVH
    score_scale = 1.0 / math.sqrt(HD)
    row_count = lax.axis_size("row")
    ctx_count = lax.axis_size("ctx")
    row_index = lax.axis_index("row")
    ctx_index = lax.axis_index("ctx")
    flat_index = ctx_index * row_count + row_index
    own_query = queries.reshape(rows_dev, step_count, KVH, groups, HD)
    slot_count, page_len, kv_width = pool_keys.shape
    slot_ids = flat_index * slot_count + jnp.arange(slot_count, dtype=jnp.int32)
    slot_match = page_table[:, :, None] == slot_ids[None, None, :]
    entry_pos = jnp.arange(page_table.shape[1], dtype=jnp.int32)
    page_of = jnp.sum(jnp.where(slot_match, entry_pos[None, :, None], 0), axis=1)
    owned = jnp.any(slot_match, axis=1)
    token_pos = (
        page_of[:, :, None] * page_len + jnp.arange(page_len, dtype=jnp.int32)[None, None, :]
    )
    live_mask = owned[:, :, None] & (token_pos < suffix_len[:, None, None])
    live_mask = live_mask.reshape(rows_dev, 1, 1, 1, slot_count * page_len)
    flat_keys = pool_keys.reshape(slot_count * page_len, KVH, HD)
    flat_values = pool_values.reshape(slot_count * page_len, KVH, HD)
    suffix_scores = (
        jnp.einsum("rskgd,tkd->rskgt", own_query, flat_keys, preferred_element_type=jnp.float32)
        * score_scale
    )
    suffix_stats = block_stats(suffix_scores, live_mask, flat_values, "rskgt,tkd->rskgd")
    fresh_keys = new_keys.reshape(rows_dev, step_count, KVH, HD)
    fresh_values = new_values.reshape(rows_dev, step_count, KVH, HD)
    fresh_scores = (
        jnp.einsum("rskgd,rtkd->rskgt", own_query, fresh_keys, preferred_element_type=jnp.float32)
        * score_scale
    )
    causal = jnp.arange(step_count)[None, :] <= jnp.arange(step_count)[:, None]
    causal = causal.reshape(1, step_count, 1, 1, step_count)
    fresh_stats = block_stats(fresh_scores, causal, fresh_values, "rskgt,rtkd->rskgd")
    query_cols = step_count * feature_width
    id_cols = jnp.broadcast_to(prefix_id.astype(jnp.bfloat16)[:, None], (rows_dev, LANES))
    packed = jnp.concatenate([queries.reshape(rows_dev, query_cols), id_cols], axis=1)
    gathered = lax.all_gather(packed, "row", axis=0, tiled=True)
    total_rows = gathered.shape[0]
    every_query = gathered[:, :query_cols].reshape(total_rows, step_count, KVH, groups, HD)
    every_prefix = gathered[:, query_cols].astype(jnp.int32)
    span_len = prefix_keys.shape[1]
    row_keys = jnp.take(prefix_keys, every_prefix, axis=0).reshape(total_rows, span_len, KVH, HD)
    row_values = jnp.take(prefix_values, every_prefix, axis=0).reshape(
        total_rows, span_len, KVH, HD
    )
    prefix_scores = (
        jnp.einsum("rskgd,rtkd->rskgt", every_query, row_keys, preferred_element_type=jnp.float32)
        * score_scale
    )
    always = jnp.ones((1, 1, 1, 1, span_len), dtype=bool)
    prefix_stats = block_stats(prefix_scores, always, row_values, "rskgt,rtkd->rskgd")
    row_start = row_index * rows_dev
    own_prefix = tuple(
        (lax.dynamic_slice_in_dim(member, row_start, rows_dev, 0) for member in prefix_stats)
    )
    own_merged = combine_pair(own_prefix, suffix_stats)
    peak_all, total_all, sum_all = tuple(
        (
            lax.dynamic_update_slice_in_dim(whole_arr, piece_arr, row_start, 0)
            for whole_arr, piece_arr in zip(prefix_stats, own_merged)
        )
    )
    units = rows_dev * step_count * H
    share = units // ctx_count
    pt_rows = -(-2 * share // LANES)
    peak_u = peak_all.reshape(row_count, ctx_count, share)
    total_u = total_all.reshape(row_count, ctx_count, share)
    sum_u = sum_all.reshape(row_count, ctx_count, share, HD)
    pt = jnp.concatenate([peak_u, total_u], axis=-1)
    pt = jnp.pad(pt, ((0, 0), (0, 0), (0, pt_rows * LANES - 2 * share)))
    pt = pt.reshape(row_count, ctx_count, pt_rows, LANES)
    outgoing = jnp.concatenate([sum_u, pt], axis=2)
    outgoing = jnp.swapaxes(outgoing, 0, 1).reshape(ctx_count * row_count, share + pt_rows, LANES)
    incoming = lax.all_to_all(outgoing, ("ctx", "row"), split_axis=0, concat_axis=0, tiled=True)
    sources = incoming.shape[0]
    got_sum = incoming[:, :share, :]
    got_pt = incoming[:, share:, :].reshape(sources, pt_rows * LANES)
    got_peak = got_pt[:, :share]
    got_total = got_pt[:, share : 2 * share]
    unit_start = ctx_index * share
    fresh_peak = lax.dynamic_slice_in_dim(fresh_stats[0].reshape(units), unit_start, share)
    fresh_total = lax.dynamic_slice_in_dim(fresh_stats[1].reshape(units), unit_start, share)
    fresh_sum = lax.dynamic_slice_in_dim(fresh_stats[2].reshape(units, HD), unit_start, share)
    top = jnp.maximum(jnp.max(got_peak, axis=0), fresh_peak)
    factor = jnp.exp(got_peak - top[None])
    fresh_factor = jnp.exp(fresh_peak - top)
    denom = jnp.sum(factor * got_total, axis=0) + fresh_factor * fresh_total
    numer = jnp.sum(factor[..., None] * got_sum, axis=0) + fresh_factor[..., None] * fresh_sum
    result = (numer / denom[..., None]).astype(jnp.bfloat16)
    whole = lax.all_gather(result, "ctx", axis=0, tiled=True)
    return whole.reshape(rows_dev, step_count, H * HD)


def solution(mesh):
    in_specs = (
        P("row", None, None),
        P("row"),
        P(None, ("ctx", "row"), None),
        P(None, ("ctx", "row"), None),
        P(("ctx", "row"), None, None),
        P(("ctx", "row"), None, None),
        P("row", None),
        P("row"),
        P("row", None, None),
        P("row", None, None),
    )
    out_specs = P("row", None, None)
    return jax.shard_map(
        per_device, mesh=mesh, in_specs=in_specs, out_specs=out_specs, check_vma=False
    )
```

profile of v0, /device:TPU:0, one launch (start us, length us, event | category | flops | bytes accessed | tf_op | source)
XLA Modules:
  0.0 77.9 jit_solution(5196668622109800049)
XLA Ops:
  0.0 0.7 convert_element_type.32
  0.7 0.8 %copy.117 = bf16[1,2,2,4096]{3,1,2,0:T(2,128)(2,1)S(1)} copy(bf16[1,2,2,4096]{3,2,1,0:T(2,128)(2,1)} %bitcast.69) | data formatting | bytes 65536
  1.6 32.5 %all-gather = bf16[8,2,8320]{2,1,0:T(2,128)(2,1)S(1)} all-gather(bf16[1,2,8320]{2,1,0:T(2,128)(2,1)S(1)} %maximum_bitcast_fusion.1), channel_id=1, replica_groups=mesh['ctx'=4,'row'=8] {'row'}, dimensions={0}, use_global_device_ids=true | all-gather | bytes 299520 | tf_op jit(solution)/shard_map/all_gather | solution.py:84
  34.5 0.7 copy-done.10
  35.1 0.2 compare_reduce_fusion
  35.3 0.2 fusion.16
  35.6 0.6 gather_fusion
  36.2 0.4 copy-done.3
  36.5 0.6 gather_fusion.1
  37.1 0.2 broadcast_select_fusion.1
  37.3 0.1 reshape.127
  37.6 0.5 fusion.22
  38.1 0.5 convert_reduce_fusion.1
  38.6 0.3 fusion.10
  39.3 0.5 copy-done.1
  39.8 0.3 reshape.130
  40.1 0.6 copy-done.11
  40.8 0.5 select_reduce_fusion
  41.4 0.9 %convert_reduce_fusion = (f32[2,2,4,8]{3,1,0,2:T(2,128)S(1)}, bf16[2,2,4,8,1024]{4,3,1,0,2:T(8,128)(2,1)}) fusion(f32[2,2,4,8,1024]{4,3,1,0,2:T(8,128)S(1)} %get-tuple-element.23, f32[2,2,4,8]{3,1,0,2:T(2,128)S(1)} %get-tuple-element.22, pred[2,1024]{1,0:T(4,128)(4,1)S(1)} %compare_and_fusion), kind=kLoop, calls=%fused_computation.22 | loop fusion | flops 655232 | bytes 789504 | tf_op jit(solution)/shard_map/reduce_sum | solution.py:19
  42.2 0.6 fusion.19
  43.2 0.3 reshape.132
  43.5 0.4 copy-done.7
  43.9 1.2 %fusion.4 = f32[16,2,4,8,128]{4,3,1,2,0:T(8,128)S(1)} fusion(f32[16,2,4,8,128]{4,3,1,2,0:T(8,128)S(1)} %copy.164, s32[]{:T(128)S(6)} %select_n.41, bf16[1024,4,128,1,1]{2,1,0,4,3:T(4,128)(2,1)S(1)} %bitcast.63, bf16[2,2,4,8,1024]{4,3,1,0,2:T(8,128)(2,1)} %get-tuple-element.16, f32[16,4,128,2,8]{2,4,3,1,0:T(8,128)S(1)} %fusion.10, ...), kind=kOutput, calls=%fused_computation.10 | convolution fusion | flops 33603584 | bytes 1458180 | tf_op jit(solution)/shard_map/rskgt,tkd->rskgd/dot_general | solution.py:20
  45.3 0.3 copy.161
  45.7 1.2 %copy.96 = f32[32,33,128]{2,1,0:T(8,128)} copy(f32[32,33,128]{2,0,1:T(8,128)S(1)} %bitcast.59) | data formatting | bytes 1081344 | tf_op jit(solution)/shard_map/reshape | solution.py:120
  46.8 5.5 %all-to-all-start = ((f32[32,33,128]{2,1,0:T(8,128)}), f32[32,33,128]{2,1,0:T(8,128)S(1)}, u32[]{:S(2)}, u32[]{:S(2)}) async-start(f32[32,33,128]{2,1,0:T(8,128)} %copy.96), calls=%async_computation | async-start | bytes 1310720 | tf_op jit(solution)/shard_map/all_to_all | solution.py:121
  52.4 0.3 select_reduce_fusion.1
  52.9 0.2 convolution_bitcast_fusion
  53.2 18.3 %all-to-all-done = f32[32,33,128]{2,1,0:T(8,128)S(1)} async-done(((f32[32,33,128]{2,1,0:T(8,128)}), f32[32,33,128]{2,1,0:T(8,128)S(1)}, u32[]{:S(2)}, u32[]{:S(2)}) %all-to-all-start) | async-done | bytes 540704 | tf_op jit(solution)/shard_map/all_to_all | solution.py:121
  71.8 0.2 fusion.8
  72.1 5.2 %all_gather.7 = bf16[128,128]{1,0:T(8,128)(2,1)S(1)} all-gather(bf16[32,128]{1,0:T(8,128)(2,1)S(1)} %divide_convert_fusion), channel_id=1, replica_groups=mesh['ctx'=4,'row'=8] {'ctx'}, dimensions={0}, use_global_device_ids=true | all-gather | bytes 40960 | tf_op jit(solution)/shard_map/all_gather | solution.py:137
  77.3 0.6 reshape.144
  (62 shorter events, 2.3 us)
Async XLA Ops:
  0.0 35.6 %copy-start = (bf16[8,32,512]{2,1,0:T(8,128)(2,1)S(1)}, bf16[8,32,512]{2,1,0:T(8,128)(2,1)}, u32[]{:S(2)}) copy-start(bf16[8,32,512]{2,1,0:T(8,128)(2,1)} %param.15) | copy-start | bytes 786436
  34.4 1.1 %copy-start.4 = (bf16[2,2,4096]{2,1,0:T(2,128)(2,1)S(1)}, bf16[2,2,4096]{2,1,0:T(2,128)(2,1)}, u32[]{:S(2)}) copy-start(bf16[2,2,4096]{2,1,0:T(2,128)(2,1)} %param.12) | copy-start | bytes 98308
  34.4 0.7 copy-start.10
  35.5 5.3 %copy-start.5 = (bf16[2,2,4,8,128]{4,3,2,1,0:T(8,128)(2,1)}, bf16[2,2,4,8,128]{4,3,2,1,0:T(8,128)(2,1)S(1)}, u32[]{:S(2)}) copy-start(bf16[2,2,4,8,128]{4,3,2,1,0:T(8,128)(2,1)S(1)} %reshape.131) | copy-start | bytes 98308
  35.6 1.0 %copy-start.3 = (bf16[8,32,512]{2,1,0:T(8,128)(2,1)S(1)}, bf16[8,32,512]{2,1,0:T(8,128)(2,1)}, u32[]{:S(2)}) copy-start(bf16[8,32,512]{2,1,0:T(8,128)(2,1)} %param.14) | copy-start | bytes 786436
  38.6 1.2 %copy-start.1 = (bf16[16,64,512]{2,1,0:T(8,128)(2,1)S(1)}, bf16[16,64,512]{2,1,0:T(8,128)(2,1)}, u32[]{:S(2)}) copy-start(bf16[16,64,512]{2,1,0:T(8,128)(2,1)} %param.16) | copy-start | bytes 3145732
  40.1 0.7 copy-start.11
  41.4 1.8 %copy-start.2 = (bf16[16,64,512]{2,1,0:T(8,128)(2,1)S(1)}, bf16[16,64,512]{2,1,0:T(8,128)(2,1)}, u32[]{:S(2)}) copy-start(bf16[16,64,512]{2,1,0:T(8,128)(2,1)} %param.17) | copy-start | bytes 3145732
  43.2 0.7 copy-start.7
  43.2 0.7 copy-start.8
  46.8 5.6 %copy-start.6 = (bf16[2,2,4,8,128]{4,3,2,1,0:T(8,128)(2,1)S(1)}, bf16[2,2,4,8,128]{4,3,2,1,0:T(8,128)(2,1)}, u32[]{:S(2)}) copy-start(bf16[2,2,4,8,128]{4,3,2,1,0:T(8,128)(2,1)} %copy-done.5) | copy-start | bytes 98308
  46.8 5.6 %copy-start.12 = (bf16[2,2,512]{2,1,0:T(2,128)(2,1)S(1)}, bf16[2,2,512]{2,1,0:T(2,128)(2,1)}, u32[]{:S(2)}) copy-start(bf16[2,2,512]{2,1,0:T(2,128)(2,1)} %param.20) | copy-start | bytes 12292
  46.8 6.1 %copy-start.9 = (bf16[2,2,512]{2,1,0:T(2,128)(2,1)S(1)}, bf16[2,2,512]{2,1,0:T(2,128)(2,1)}, u32[]{:S(2)}) copy-start(bf16[2,2,512]{2,1,0:T(2,128)(2,1)} %param.21) | copy-start | bytes 12292
  46.8 24.7 %all-to-all-start = ((f32[32,33,128]{2,1,0:T(8,128)}), f32[32,33,128]{2,1,0:T(8,128)S(1)}, u32[]{:S(2)}, u32[]{:S(2)}) async-start(f32[32,33,128]{2,1,0:T(8,128)} %copy.96), calls=%async_computation | async-start | bytes 1310720 | tf_op jit(solution)/shard_map/all_to_all | solution.py:121
where the time goes:
time: 78.4 us; the launch traced here: 77.9 us
  blocking collectives  37.7 us (48%)
  waiting for transfers between devices  18.3 us (23%)
  local copies, waits for them, and re-layouts  8.64 us (11%)
  starting transfers between devices  5.54 us (7%)
  other arithmetic  4.24 us (5%)
  matrix products  3.09 us (4%)
    all_gather x1, blocking collectives, per_device(): gathered = lax.all_gather(packed, 'row', axis=0, tiled=True)  32.5 us
    all_to_all x1, waiting for transfers between devices, per_device(): lax.all_to_all(outgoing, ('ctx', 'row'), split_axis=0, concat_axis=0, til...  18.3 us
    all_to_all x1, starting transfers between devices, per_device(): lax.all_to_all(outgoing, ('ctx', 'row'), split_axis=0, concat_axis=0, til...  5.54 us
    all_gather x1, blocking collectives, per_device(): whole = lax.all_gather(result, 'ctx', axis=0, tiled=True)  5.18 us
    unnamed x31, local copies, waits for them, and re-layouts  3.59 us
    dot_general x3, matrix products, block_stats(): jnp.einsum(einsum_form, weights, values, preferred_element_type=jnp.float32)  1.75 us
  transfers between devices with their start and end apart: 1, of which 1 were waited for; matrix products, arithmetic and copies ran while one was open for 1% of the time, Pallas kernels for 0%

commit v1 on v0

--- a/solution.py
+++ b/solution.py
@@ -81,7 +81,12 @@
     query_cols = step_count * feature_width
     id_cols = jnp.broadcast_to(prefix_id.astype(jnp.bfloat16)[:, None], (rows_dev, LANES))
     packed = jnp.concatenate([queries.reshape(rows_dev, query_cols), id_cols], axis=1)
-    gathered = lax.all_gather(packed, "row", axis=0, tiled=True)
+    ring = [packed]
+    for hop in range(7):
+        ring.append(lax.ppermute(ring[-1], "row", [(dev, (dev + 1) % 8) for dev in range(8)]))
+    gathered = jnp.roll(
+        jnp.concatenate(ring[::-1], axis=0), (lax.axis_index("row") + 1) * ring[0].shape[0], axis=0
+    )
     total_rows = gathered.shape[0]
     every_query = gathered[:, :query_cols].reshape(total_rows, step_count, KVH, groups, HD)
     every_prefix = gathered[:, query_cols].astype(jnp.int32)

time: 78.4 us -> 88.3 us (1.13)
  waiting for transfers between devices: 18.3 us -> 59.1 us
  blocking collectives: 37.7 us -> 5.18 us
  local copies, waits for them, and re-layouts: 8.64 us -> 12.4 us
  other arithmetic: 4.24 us -> 3.12 us
  matrix products: 3.09 us -> 2.14 us
    ppermute x0 -> x7, waiting for transfers between devices: none -> 40.7 us  [per_device(): lax.ppermute(ring[-1], 'row', [(dev, (dev + 1) % 8) for dev in range(8)])]
    all_gather x1 -> x0, blocking collectives: 32.5 us -> none  [per_device(): gathered = lax.all_gather(packed, 'row', axis=0, tiled=True)]
    concatenate x0 -> x1, local copies, waits for them, and re-layouts: none -> 3.19 us  [per_device(): jnp.roll(jnp.concatenate(ring[::-1], axis=0), (lax.axis_index('row') + 1)...]
    ppermute x0 -> x7, starting transfers between devices: none -> 3.01 us  [per_device(): lax.ppermute(ring[-1], 'row', [(dev, (dev + 1) % 8) for dev in range(8)])]
    all_to_all x1, starting transfers between devices: 5.54 us -> 2.75 us  [per_device(): lax.all_to_all(outgoing, ('ctx', 'row'), split_axis=0, concat_axis=0, til...]
    unnamed x31 -> x22, local copies, waits for them, and re-layouts: 3.59 us -> 2.23 us
    reshape x1, local copies, waits for them, and re-layouts: 0.27 us -> 1.35 us  [per_device(): flat_keys = pool_keys.reshape(slot_count * page_len, KVH, HD)]
    dot_general x3, matrix products: 1.75 us -> 0.81 us  [block_stats(): jnp.einsum(einsum_form, weights, values, preferred_element_type=jnp.float32)]
  transfers between devices with their start and end apart: 1 -> 8, of which waited for: 1 -> 8; matrix products, arithmetic and copies ran while one was open for 1% -> 6% of each run, Pallas kernels for 0% -> 0%
where the time goes in v1:
time: 88.3 us; the launch traced here: 88 us
  waiting for transfers between devices  59.1 us (67%)
  local copies, waits for them, and re-layouts  12.4 us (14%)
  starting transfers between devices  5.75 us (7%)
  blocking collectives  5.18 us (6%)
  other arithmetic  3.12 us (4%)
  matrix products  2.14 us (2%)
    ppermute x7, waiting for transfers between devices, per_device(): lax.ppermute(ring[-1], 'row', [(dev, (dev + 1) % 8) for dev in range(8)])  40.7 us
    all_to_all x1, waiting for transfers between devices, per_device(): lax.all_to_all(outgoing, ('ctx', 'row'), split_axis=0, concat_axis=0, til...  18.3 us
    all_gather x1, blocking collectives, per_device(): whole = lax.all_gather(result, 'ctx', axis=0, tiled=True)  5.18 us
    concatenate x1, local copies, waits for them, and re-layouts, per_device(): jnp.roll(jnp.concatenate(ring[::-1], axis=0), (lax.axis_index('row') + 1)...  3.19 us
    ppermute x7, starting transfers between devices, per_device(): lax.ppermute(ring[-1], 'row', [(dev, (dev + 1) % 8) for dev in range(8)])  3.01 us
    all_to_all x1, starting transfers between devices, per_device(): lax.all_to_all(outgoing, ('ctx', 'row'), split_axis=0, concat_axis=0, til...  2.75 us
    unnamed x22, local copies, waits for them, and re-layouts  2.23 us
  transfers between devices with their start and end apart: 8, of which 8 were waited for; matrix products, arithmetic and copies ran while one was open for 6% of the time, Pallas kernels for 0%

profile of v1, /device:TPU:0, one launch (start us, length us, event | category | flops | bytes accessed | tf_op | source)
XLA Modules:
  0.0 88.0 jit_solution(12798678446265952516)
XLA Ops:
  0.0 0.7 convert_element_type.32
  0.7 0.8 copy.117
  1.6 3.0 %collective-permute-start = (bf16[2,8320]{1,0:T(2,128)(2,1)S(1)}, bf16[2,8320]{1,0:T(2,128)(2,1)S(1)}, u32[]{:S(2)}, u32[]{:S(2)}) collective-permute-start(bf16[2,8320]{1,0:T(2,128)(2,1)S(1)} %pad_maximum_fusion), channel_id=1, source_target_pairs={{0,1},{1,2},{2,3},{3,4},{4,5},{5,6},{6,7},{7,0},{8,9},{9,10},{10,1... | collective-permute-start | bytes 99848 | tf_op jit(solution)/shard_map/ppermute | solution.py:86
  4.6 4.9 %collective-permute-done = bf16[2,8320]{1,0:T(2,128)(2,1)S(1)} collective-permute-done((bf16[2,8320]{1,0:T(2,128)(2,1)S(1)}, bf16[2,8320]{1,0:T(2,128)(2,1)S(1)}, u32[]{:S(2)}, u32[]{:S(2)}) %collective-permute-start) | collective-permute-done | bytes 33312 | tf_op jit(solution)/shard_map/ppermute | solution.py:86
  9.7 6.4 %collective-permute-done.1 = bf16[2,8320]{1,0:T(2,128)(2,1)S(1)} collective-permute-done((bf16[2,8320]{1,0:T(2,128)(2,1)S(1)}, bf16[2,8320]{1,0:T(2,128)(2,1)S(1)}, u32[]{:S(2)}, u32[]{:S(2)}) %collective-permute-start.1) | collective-permute-done | bytes 33312 | tf_op jit(solution)/shard_map/ppermute | solution.py:86
  16.2 6.6 %collective-permute-done.2 = bf16[2,8320]{1,0:T(2,128)(2,1)S(1)} collective-permute-done((bf16[2,8320]{1,0:T(2,128)(2,1)S(1)}, bf16[2,8320]{1,0:T(2,128)(2,1)S(1)}, u32[]{:S(2)}, u32[]{:S(2)}) %collective-permute-start.2) | collective-permute-done | bytes 33312 | tf_op jit(solution)/shard_map/ppermute | solution.py:86
  23.4 6.0 %collective-permute-done.3 = bf16[2,8320]{1,0:T(2,128)(2,1)S(1)} collective-permute-done((bf16[2,8320]{1,0:T(2,128)(2,1)S(1)}, bf16[2,8320]{1,0:T(2,128)(2,1)S(1)}, u32[]{:S(2)}, u32[]{:S(2)}) %collective-permute-start.3) | collective-permute-done | bytes 33312 | tf_op jit(solution)/shard_map/ppermute | solution.py:86
  29.5 1.3 %reshape.130 = bf16[1024,4,128]{2,1,0:T(4,128)(2,1)S(1)} reshape(bf16[16,64,512]{2,1,0:T(8,128)(2,1)} %param.16) | data formatting | bytes 2097152 | tf_op jit(solution)/shard_map/reshape | solution.py:65
  30.9 5.5 %collective-permute-done.4 = bf16[2,8320]{1,0:T(2,128)(2,1)S(1)} collective-permute-done((bf16[2,8320]{1,0:T(2,128)(2,1)S(1)}, bf16[2,8320]{1,0:T(2,128)(2,1)S(1)}, u32[]{:S(2)}, u32[]{:S(2)}) %collective-permute-start.4) | collective-permute-done | bytes 33312 | tf_op jit(solution)/shard_map/ppermute | solution.py:86
  36.4 0.5 select_reduce_fusion
  36.9 6.1 %collective-permute-done.5 = bf16[2,8320]{1,0:T(2,128)(2,1)S(1)} collective-permute-done((bf16[2,8320]{1,0:T(2,128)(2,1)S(1)}, bf16[2,8320]{1,0:T(2,128)(2,1)S(1)}, u32[]{:S(2)}, u32[]{:S(2)}) %collective-permute-start.5) | collective-permute-done | bytes 33312 | tf_op jit(solution)/shard_map/ppermute | solution.py:86
  43.0 0.3 convert_reduce_fusion
  43.2 1.1 %reshape.132 = bf16[1024,4,128]{2,1,0:T(4,128)(2,1)} reshape(bf16[16,64,512]{2,1,0:T(8,128)(2,1)S(1)} %copy-done.1) | data formatting | bytes 2097152 | tf_op jit(solution)/shard_map/reshape | solution.py:66
  44.4 5.2 %collective-permute-done.6 = bf16[2,8320]{1,0:T(2,128)(2,1)S(1)} collective-permute-done((bf16[2,8320]{1,0:T(2,128)(2,1)S(1)}, bf16[2,8320]{1,0:T(2,128)(2,1)S(1)}, u32[]{:S(2)}, u32[]{:S(2)}) %collective-permute-start.6) | collective-permute-done | bytes 33312 | tf_op jit(solution)/shard_map/ppermute | solution.py:86
  49.6 3.2 %concatenate.16 = bf16[32,8320]{1,0:T(8,128)(2,1)S(1)} concatenate(bf16[2,8320]{1,0:T(2,128)(2,1)S(1)} %collective-permute-done.6, bf16[2,8320]{1,0:T(2,128)(2,1)S(1)} %collective-permute-done.5, bf16[2,8320]{1,0:T(2,128)(2,1)S(1)} %collective-permute-done.4, bf16[2,8320]{1,0:T(2,128)(2,1)S(1)} %collective-permute-done.3, bf16[2,8320]{1,0:T(2,128)(2,1)S(1)} %collective-permute-done.2, ...), dimensions={0} | concatenate | bytes 1064960 | tf_op jit(solution)/shard_map/jit(_roll_dynamic)/concatenate | solution.py:87
  52.8 0.2 convert_reduce_fusion.3
  53.1 0.6 gather_fusion
  53.7 0.4 copy-done.3
  54.1 0.6 gather_fusion.1
  55.1 0.5 fusion.22
  55.7 0.5 convert_reduce_fusion.1
  56.1 0.3 fusion.10
  56.8 0.9 %copy-done.2 = bf16[1024,4,128]{2,1,0:T(4,128)(2,1)S(1)} copy-done((bf16[1024,4,128]{2,1,0:T(4,128)(2,1)S(1)}, bf16[1024,4,128]{2,1,0:T(4,128)(2,1)}, u32[]{:S(2)}) %copy-start.2) | copy-done | bytes 1048600
  57.7 0.3 fusion.4
  58.2 0.3 copy.161
  58.5 1.2 %copy.96 = f32[32,33,128]{2,1,0:T(8,128)} copy(f32[32,33,128]{2,0,1:T(8,128)S(1)} %bitcast.57) | data formatting | bytes 1081344 | tf_op jit(solution)/shard_map/reshape | solution.py:125
  59.7 2.7 %all-to-all-start = ((f32[32,33,128]{2,1,0:T(8,128)}), f32[32,33,128]{2,1,0:T(8,128)S(1)}, u32[]{:S(2)}, u32[]{:S(2)}) async-start(f32[32,33,128]{2,1,0:T(8,128)} %copy.96), calls=%async_computation | async-start | bytes 1310720 | tf_op jit(solution)/shard_map/all_to_all | solution.py:126
  62.4 0.3 select_reduce_fusion.1
  63.2 18.3 %all-to-all-done = f32[32,33,128]{2,1,0:T(8,128)S(1)} async-done(((f32[32,33,128]{2,1,0:T(8,128)}), f32[32,33,128]{2,1,0:T(8,128)S(1)}, u32[]{:S(2)}, u32[]{:S(2)}) %all-to-all-start) | async-done | bytes 540704 | tf_op jit(solution)/shard_map/all_to_all | solution.py:126
  81.9 0.2 fusion.8
  82.2 5.2 %all_gather.3 = bf16[128,128]{1,0:T(8,128)(2,1)S(1)} all-gather(bf16[32,128]{1,0:T(8,128)(2,1)S(1)} %divide_convert_fusion), channel_id=1, replica_groups=mesh['ctx'=4,'row'=8] {'ctx'}, dimensions={0}, use_global_device_ids=true | all-gather | bytes 40960 | tf_op jit(solution)/shard_map/all_gather | solution.py:142
  87.3 0.6 reshape.144
  (67 shorter events, 3.0 us)
Async XLA Ops:
  0.0 53.1 %copy-start = (bf16[8,32,512]{2,1,0:T(8,128)(2,1)S(1)}, bf16[8,32,512]{2,1,0:T(8,128)(2,1)}, u32[]{:S(2)}) copy-start(bf16[8,32,512]{2,1,0:T(8,128)(2,1)} %param.15) | copy-start | bytes 786436
  1.6 7.9 %collective-permute-start = (bf16[2,8320]{1,0:T(2,128)(2,1)S(1)}, bf16[2,8320]{1,0:T(2,128)(2,1)S(1)}, u32[]{:S(2)}, u32[]{:S(2)}) collective-permute-start(bf16[2,8320]{1,0:T(2,128)(2,1)S(1)} %pad_maximum_fusion), channel_id=1, source_target_pairs={{0,1},{1,2},{2,3},{3,4},{4,5},{5,6},{6,7},{7,0},{8,9},{9,10},{10,1... | collective-permute-start | bytes 99848 | tf_op jit(solution)/shard_map/ppermute | solution.py:86
  4.6 4.9 %copy-start.6 = (s32[2,32]{1,0:T(2,128)S(1)}, s32[2,32]{1,0:T(2,128)}, u32[]{:S(2)}) copy-start(s32[2,32]{1,0:T(2,128)} %param.18) | copy-start | bytes 772
  9.5 6.6 %collective-permute-start.1 = (bf16[2,8320]{1,0:T(2,128)(2,1)S(1)}, bf16[2,8320]{1,0:T(2,128)(2,1)S(1)}, u32[]{:S(2)}, u32[]{:S(2)}) collective-permute-start(bf16[2,8320]{1,0:T(2,128)(2,1)S(1)} %collective-permute-done), channel_id=1, source_target_pairs={{0,1},{1,2},{2,3},{3,4},{4,5},{5,6},{6,7},{7,0},{8,9},{9,10},{10,1... | collective-permute-start | bytes 99848 | tf_op jit(solution)/shard_map/ppermute | solution.py:86
  16.2 6.6 %collective-permute-start.2 = (bf16[2,8320]{1,0:T(2,128)(2,1)S(1)}, bf16[2,8320]{1,0:T(2,128)(2,1)S(1)}, u32[]{:S(2)}, u32[]{:S(2)}) collective-permute-start(bf16[2,8320]{1,0:T(2,128)(2,1)S(1)} %collective-permute-done.1), channel_id=1, source_target_pairs={{0,1},{1,2},{2,3},{3,4},{4,5},{5,6},{6,7},{7,0},{8,9},{9,10},{10,1... | collective-permute-start | bytes 99848 | tf_op jit(solution)/shard_map/ppermute | solution.py:86
  22.8 6.6 %collective-permute-start.3 = (bf16[2,8320]{1,0:T(2,128)(2,1)S(1)}, bf16[2,8320]{1,0:T(2,128)(2,1)S(1)}, u32[]{:S(2)}, u32[]{:S(2)}) collective-permute-start(bf16[2,8320]{1,0:T(2,128)(2,1)S(1)} %collective-permute-done.2), channel_id=1, source_target_pairs={{0,1},{1,2},{2,3},{3,4},{4,5},{5,6},{6,7},{7,0},{8,9},{9,10},{10,1... | collective-permute-start | bytes 99848 | tf_op jit(solution)/shard_map/ppermute | solution.py:86
  23.2 6.3 %copy-start.4 = (bf16[2,2,4096]{2,1,0:T(2,128)(2,1)S(1)}, bf16[2,2,4096]{2,1,0:T(2,128)(2,1)}, u32[]{:S(2)}) copy-start(bf16[2,2,4096]{2,1,0:T(2,128)(2,1)} %param.12) | copy-start | bytes 98308
  23.3 6.1 %copy-start.7 = (s32[2]{0:T(128)S(1)}, s32[2]{0:T(128)}, u32[]{:S(2)}) copy-start(s32[2]{0:T(128)} %param.19) | copy-start | bytes 28
  29.4 7.0 %collective-permute-start.4 = (bf16[2,8320]{1,0:T(2,128)(2,1)S(1)}, bf16[2,8320]{1,0:T(2,128)(2,1)S(1)}, u32[]{:S(2)}, u32[]{:S(2)}) collective-permute-start(bf16[2,8320]{1,0:T(2,128)(2,1)S(1)} %collective-permute-done.3), channel_id=1, source_target_pairs={{0,1},{1,2},{2,3},{3,4},{4,5},{5,6},{6,7},{7,0},{8,9},{9,10},{10,1... | collective-permute-start | bytes 99848 | tf_op jit(solution)/shard_map/ppermute | solution.py:86
  36.3 6.6 %collective-permute-start.5 = (bf16[2,8320]{1,0:T(2,128)(2,1)S(1)}, bf16[2,8320]{1,0:T(2,128)(2,1)S(1)}, u32[]{:S(2)}, u32[]{:S(2)}) collective-permute-start(bf16[2,8320]{1,0:T(2,128)(2,1)S(1)} %collective-permute-done.4), channel_id=1, source_target_pairs={{0,1},{1,2},{2,3},{3,4},{4,5},{5,6},{6,7},{7,0},{8,9},{9,10},{10,1... | collective-permute-start | bytes 99848 | tf_op jit(solution)/shard_map/ppermute | solution.py:86
  36.4 6.9 %copy-start.1 = (bf16[16,64,512]{2,1,0:T(8,128)(2,1)S(1)}, bf16[16,64,512]{2,1,0:T(8,128)(2,1)}, u32[]{:S(2)}) copy-start(bf16[16,64,512]{2,1,0:T(8,128)(2,1)} %param.17) | copy-start | bytes 3145732
  43.0 6.6 %collective-permute-start.6 = (bf16[2,8320]{1,0:T(2,128)(2,1)S(1)}, bf16[2,8320]{1,0:T(2,128)(2,1)S(1)}, u32[]{:S(2)}, u32[]{:S(2)}) collective-permute-start(bf16[2,8320]{1,0:T(2,128)(2,1)S(1)} %collective-permute-done.5), channel_id=1, source_target_pairs={{0,1},{1,2},{2,3},{3,4},{4,5},{5,6},{6,7},{7,0},{8,9},{9,10},{10,1... | collective-permute-start | bytes 99848 | tf_op jit(solution)/shard_map/ppermute | solution.py:86
  53.1 1.0 %copy-start.3 = (bf16[8,32,512]{2,1,0:T(8,128)(2,1)S(1)}, bf16[8,32,512]{2,1,0:T(8,128)(2,1)}, u32[]{:S(2)}) copy-start(bf16[8,32,512]{2,1,0:T(8,128)(2,1)} %param.14) | copy-start | bytes 786436
  56.4 1.2 %copy-start.2 = (bf16[1024,4,128]{2,1,0:T(4,128)(2,1)S(1)}, bf16[1024,4,128]{2,1,0:T(4,128)(2,1)}, u32[]{:S(2)}) copy-start(bf16[1024,4,128]{2,1,0:T(4,128)(2,1)} %reshape.132) | copy-start | bytes 3145732
  59.7 2.8 %copy-start.8 = (bf16[2,2,512]{2,1,0:T(2,128)(2,1)S(1)}, bf16[2,2,512]{2,1,0:T(2,128)(2,1)}, u32[]{:S(2)}) copy-start(bf16[2,2,512]{2,1,0:T(2,128)(2,1)} %param.20) | copy-start | bytes 12292
  59.7 3.3 %copy-start.5 = (bf16[2,2,512]{2,1,0:T(2,128)(2,1)S(1)}, bf16[2,2,512]{2,1,0:T(2,128)(2,1)}, u32[]{:S(2)}) copy-start(bf16[2,2,512]{2,1,0:T(2,128)(2,1)} %param.21) | copy-start | bytes 12292
  59.7 21.9 %all-to-all-start = ((f32[32,33,128]{2,1,0:T(8,128)}), f32[32,33,128]{2,1,0:T(8,128)S(1)}, u32[]{:S(2)}, u32[]{:S(2)}) async-start(f32[32,33,128]{2,1,0:T(8,128)} %copy.96), calls=%async_computation | async-start | bytes 1310720 | tf_op jit(solution)/shard_map/all_to_all | solution.py:126
